TPU v7x, 256 devices: a whole 4x4x8 slice. The times are simulated.
256 devices in a mesh: vel: 16 (over y, z_lo), space: 16 (over x, z_hi, core).
Axes of the slice: x: 4, y: 4, z: 8 (z_hi: 2, z_lo: 4; z = z_hi * 4 + z_lo), core: 2. Of those that a mesh axis runs over, the one named last changes fastest.
Arguments:
- initial: float32 [13824, 64, 128], P('vel', 'space'), as said below
- site_kind: int32 [64, 128], P('space'), may hold values from 0 to 2, as said below
Outputs:
- distribution: float32 [13824, 64, 128], P('vel', 'space')
- kelvin_level: float32 [64, 128], P('space')
Inputs may be any that keep to these rules, and one draw needn't show every extreme that they name: `site_kind`: 0 marks a gas cell, 1 a wall cell, 2 an inflow cell. `initial`: every entry is positive.
All inputs are finite; a program needn't handle non-finite values.
Results may differ from a plain program's by a relative error of at most 0.0003.
Values sent between devices are 32-bit elements; how exact they have to be, the bound alone decides.
No kernel may reach another device: no remote copies, remote signals or barrier semaphores. Data moves between devices by JAX's collectives and lax.ppermute only.
A program may use at most 64 MiB of HBM per device.

v0:
```python
import math
import jax
import jax.numpy as jnp
from jax import lax
from jax.sharding import PartitionSpec as P

NVX = 24
STEPS = 2
speed_limit = 4.0
courant = 0.1
diffusivity_ratio = 2.0 / 3.0
power_law_index = 0.81
encounter_rate = 0.25
wall_kelvin = 1.0
inflow_concentration = 1.0
inflow_speed = 0.5
inflow_kelvin = 1.0


def with_halo(block, sides, width):
    for axis, dim in sides:
        count = lax.axis_size(axis)
        forward = [(i, i + 1) for i in range(count - 1)]
        backward = [(target, source) for source, target in forward]
        low = lax.ppermute(
            lax.slice_in_dim(block, block.shape[dim] - width, None, axis=dim), axis, forward
        )
        high = lax.ppermute(lax.slice_in_dim(block, 0, width, axis=dim), axis, backward)
        block = jnp.concatenate([low, block, high], axis=dim)
    return block


def speeds(offset, amount):
    index = offset + jnp.arange(amount, dtype=jnp.int32)
    spacing = 2.0 * speed_limit / (NVX - 1)
    along_x_part = -speed_limit + spacing * (index // (NVX * NVX)).astype(jnp.float32)
    along_y_part = -speed_limit + spacing * (index // NVX % NVX).astype(jnp.float32)
    along_z_part = -speed_limit + spacing * (index % NVX).astype(jnp.float32)
    return (along_x_part, along_y_part, along_z_part)


def quad_weight():
    return (2.0 * speed_limit / (NVX - 1)) ** 3 / (2.0 * math.pi) ** 1.5


def minmod(left, right):
    return 0.5 * (jnp.sign(left) + jnp.sign(right)) * jnp.minimum(jnp.abs(left), jnp.abs(right))


def sweep(distribution_table, number, along):
    length = distribution_table.shape[along]

    def piece(source, low, high):
        return lax.slice_in_dim(source, low, high, axis=along)

    jumps = piece(distribution_table, 1, length) - piece(distribution_table, 0, length - 1)
    slopes = minmod(piece(jumps, 0, length - 2), piece(jumps, 1, length - 1))
    left_face = piece(distribution_table, 1, length - 2) + 0.5 * (1.0 - number) * piece(
        slopes, 0, length - 3
    )
    right_face = piece(distribution_table, 2, length - 1) - 0.5 * (1.0 + number) * piece(
        slopes, 1, length - 2
    )
    flux = number * jnp.where(number > 0, left_face, right_face)
    return piece(distribution_table, 2, length - 2) - (
        piece(flux, 1, length - 3) - piece(flux, 0, length - 4)
    )


def transport(padded, along_x_part, along_y_part):
    swept = sweep(padded, courant * along_x_part[:, None, None], 1)
    widened = jnp.pad(swept, ((0, 0), (0, 0), (2, 2)))
    return sweep(widened, courant * along_y_part[:, None, None], 2)


def macroscopic_moments(advected_distribution, along_x_part, along_y_part, along_z_part):
    magnitude_squares = (
        along_x_part * along_x_part + along_y_part * along_y_part + along_z_part * along_z_part
    )
    ones = jnp.ones_like(along_x_part)
    table = quad_weight() * jnp.stack(
        [ones, along_x_part, along_y_part, along_z_part, magnitude_squares]
    )
    local = jnp.einsum("kv,vrc->krc", table, advected_distribution, precision=lax.Precision.HIGHEST)
    integral_totals = lax.psum(local, "vel")
    particle_concentration = integral_totals[0]
    average_drift_x = integral_totals[1] / particle_concentration
    average_drift_y = integral_totals[2] / particle_concentration
    average_drift_z = integral_totals[3] / particle_concentration
    kelvin_level = (
        integral_totals[4] / particle_concentration
        - (
            average_drift_x * average_drift_x
            + average_drift_y * average_drift_y
            + average_drift_z * average_drift_z
        )
    ) / 3.0
    rel_x = along_x_part[:, None, None] - average_drift_x[None]
    rel_y = along_y_part[:, None, None] - average_drift_y[None]
    rel_z = along_z_part[:, None, None] - average_drift_z[None]
    scaled = (
        0.5
        * quad_weight()
        * (rel_x * rel_x + rel_y * rel_y + rel_z * rel_z)
        * advected_distribution
    )
    local_heat = jnp.stack(
        [
            jnp.sum(rel_x * scaled, axis=0),
            jnp.sum(rel_y * scaled, axis=0),
            jnp.sum(rel_z * scaled, axis=0),
        ]
    )
    conductive_transfer = lax.psum(local_heat, "vel")
    return (
        particle_concentration,
        average_drift_x,
        average_drift_y,
        average_drift_z,
        kelvin_level,
        conductive_transfer,
    )


def approach_increment(
    advected_distribution, kind_labels, along_x_part, along_y_part, along_z_part
):
    (
        particle_concentration,
        average_drift_x,
        average_drift_y,
        average_drift_z,
        kelvin_level,
        conductive_transfer,
    ) = macroscopic_moments(advected_distribution, along_x_part, along_y_part, along_z_part)
    rel_x = along_x_part[:, None, None] - average_drift_x[None]
    rel_y = along_y_part[:, None, None] - average_drift_y[None]
    rel_z = along_z_part[:, None, None] - average_drift_z[None]
    relative_magnitude_square = rel_x * rel_x + rel_y * rel_y + rel_z * rel_z
    stress_scalar_grid = particle_concentration * kelvin_level
    gaussian_local_balance = (
        particle_concentration
        * kelvin_level ** (-1.5)
        * jnp.exp(-relative_magnitude_square / (2.0 * kelvin_level))
    )
    conductive_vector_slot = (
        rel_x * conductive_transfer[0]
        + rel_y * conductive_transfer[1]
        + rel_z * conductive_transfer[2]
    )
    corrected_goal_distribution = gaussian_local_balance * (
        1.0
        + (1.0 - diffusivity_ratio)
        * conductive_vector_slot
        * (relative_magnitude_square / kelvin_level - 5.0)
        / (5.0 * stress_scalar_grid * kelvin_level)
    )
    approach_rate = (
        encounter_rate * particle_concentration * kelvin_level ** (1.0 - power_law_index)
    )
    relaxed = advected_distribution + approach_rate * (
        corrected_goal_distribution - advected_distribution
    )
    magnitude_squares = (
        along_x_part * along_x_part + along_y_part * along_y_part + along_z_part * along_z_part
    )[:, None, None]
    wall_distribution = (
        particle_concentration
        * wall_kelvin ** (-1.5)
        * jnp.exp(-magnitude_squares / (2.0 * wall_kelvin))
    )
    inflow_magnitude_square = (
        (along_x_part - inflow_speed) ** 2
        + along_y_part * along_y_part
        + along_z_part * along_z_part
    )[:, None, None]
    inflow_distribution = (
        inflow_concentration
        * inflow_kelvin ** (-1.5)
        * jnp.exp(-inflow_magnitude_square / (2.0 * inflow_kelvin))
    )
    revised_distribution = jnp.where(
        kind_labels == 1,
        wall_distribution,
        jnp.where(kind_labels == 2, inflow_distribution, relaxed),
    )
    return (revised_distribution, kelvin_level)


def per_device(initial, site_kind):
    amount = initial.shape[0]
    along_x_part, along_y_part, along_z_part = speeds(lax.axis_index("vel") * amount, amount)
    distribution_table = initial
    kelvin_level = jnp.zeros(site_kind.shape, jnp.float32)
    for section in range(STEPS):
        padded = with_halo(distribution_table, (("space", 1),), 2)
        advected_distribution = transport(padded, along_x_part, along_y_part)
        distribution_table, kelvin_level = approach_increment(
            advected_distribution, site_kind, along_x_part, along_y_part, along_z_part
        )
    return (distribution_table, kelvin_level)


def solution(mesh):
    return jax.shard_map(
        per_device,
        mesh=mesh,
        in_specs=(P("vel", "space", None), P("space", None)),
        out_specs=(P("vel", "space", None), P("space", None)),
        check_vma=False,
    )
```

profile of v0, /device:TPU:38, one launch (start us, length us, event | category | flops | bytes accessed | tf_op | source)
XLA Modules:
  0.0 373.0 jit_solution(16900406047952305739)
XLA Ops:
  0.6 1.6 copy.19
  2.2 1.3 fusion.116
  3.5 8.0 %collective-permute-start.1 = (f32[864,2,128]{2,0,1:T(8,128)}, f32[864,2,128]{2,0,1:T(8,128)}, u32[]{:S(2)}, u32[]{:S(2)}) collective-permute-start(f32[864,2,128]{2,0,1:T(8,128)} %get-tuple-element.21), channel_id=1, source_target_pairs={{1,0},{2,1},{3,2},{4,3},{5,4},{6,5},{7,6},{8,7},{9,8},{10,9},{11,1... | collective-permute-start | bytes 2654216 | tf_op jit(solution)/shard_map/ppermute | solution.py:28
  11.6 1.9 collective-permute-start
  13.5 0.1 multiply_add_fusion
  13.7 0.6 add_multiply_fusion.1
  14.3 0.6 broadcast.950
  14.9 1.3 stack.36
  16.3 0.6 multiply_exponential_fusion
  17.0 1.3 broadcast_compare_fusion.3
  18.3 33.8 %collective-permute-done = f32[864,2,128]{2,0,1:T(8,128)} collective-permute-done((f32[864,2,128]{2,0,1:T(8,128)}, f32[864,2,128]{2,0,1:T(8,128)}, u32[]{:S(2)}, u32[]{:S(2)}) %collective-permute-start) | collective-permute-done | bytes 884768 | tf_op jit(solution)/shard_map/ppermute | solution.py:25
  52.1 1.2 constant_dynamic-update-slice_fusion.2
  53.3 0.1 constant_dynamic-update-slice_fusion.1
  53.4 1.2 constant_dynamic-update-slice_fusion
  54.7 0.2 slice_subtract_fusion.1
  54.9 1.1 minimum_multiply_fusion.3
  56.1 2.0 fusion.16
  58.1 0.2 fusion.71
  58.3 1.9 fusion.3
  60.2 2.4 minimum_multiply_fusion.1
  62.7 2.6 fusion.2
  65.3 0.5 fusion.70
  65.8 0.2 copy-done.1
  66.0 0.9 fusion.74
  67.0 70.9 %psum.28 = f32[5,4,128]{2,0,1:T(8,128)S(1)} all-reduce(f32[5,4,128]{2,0,1:T(8,128)S(1)} %fusion.74), channel_id=1, replica_groups=mesh['vel'=16,'space'=16] {'vel'}, use_global_device_ids=true, to_apply=%region_0.1 | all-reduce | flops 2560 | bytes 20480 | tf_op jit(solution)/shard_map/psum | solution.py:85
  137.9 1.1 fusion.20
  139.1 44.3 %psum.29 = f32[3,4,128]{2,1,0:T(4,128)S(1)} all-reduce(f32[3,4,128]{2,1,0:T(4,128)S(1)} %pad_maximum_fusion.5), channel_id=1, replica_groups=mesh['vel'=16,'space'=16] {'vel'}, use_global_device_ids=true, to_apply=%region_4.5 | all-reduce | flops 1536 | bytes 12288 | tf_op jit(solution)/shard_map/psum | solution.py:114
  183.4 4.3 %fusion.42 = f32[864,4,128]{2,0,1:T(8,128)S(1)} fusion(f32[864,4,128]{2,0,1:T(8,128)S(1)} %fusion.70, f32[4,128]{1,0:T(4,128)S(1)} %bitcast.109, f32[4,128]{1,0:T(4,128)S(1)} %bitcast.115, f32[4,128]{1,0:T(4,128)S(1)} %get-tuple-element.37, f32[4,128]{1,0:T(4,128)S(1)} %get-tuple-element.38, f32[4,128]{1,0:T(4,128)S(1)} %get-tuple-element.36, ...), kind=kLoop, calls=%fused_computation.87 | loop fusion | flops 12828672 | bytes 3581824 | tf_op jit(solution)/shard_map/jit(_where)/select_n | solution.py:182
  187.7 0.1 fusion.115
  187.8 1.9 collective-permute-start.2
  189.8 8.4 %collective-permute-start.3 = (f32[864,2,128]{2,0,1:T(8,128)S(1)}, f32[864,2,128]{2,0,1:T(8,128)S(1)}, u32[]{:S(2)}, u32[]{:S(2)}) collective-permute-start(f32[864,2,128]{2,0,1:T(8,128)S(1)} %get-tuple-element.20), channel_id=1, source_target_pairs={{1,0},{2,1},{3,2},{4,3},{5,4},{6,5},{7,6},{8,7},{9,8},{10,9},{11,1... | collective-permute-start | bytes 2654216 | tf_op jit(solution)/shard_map/ppermute | solution.py:28
  198.2 34.0 %collective-permute-done.2 = f32[864,2,128]{2,0,1:T(8,128)S(1)} collective-permute-done((f32[864,2,128]{2,0,1:T(8,128)S(1)}, f32[864,2,128]{2,0,1:T(8,128)S(1)}, u32[]{:S(2)}, u32[]{:S(2)}) %collective-permute-start.2) | collective-permute-done | bytes 884768 | tf_op jit(solution)/shard_map/ppermute | solution.py:25
  232.2 0.2 pad_maximum_fusion
  232.4 0.2 slice_subtract_fusion
  232.7 1.1 minimum_multiply_fusion.2
  233.9 1.0 fusion.12
  234.9 3.8 %fusion.69 = f32[864,4,128]{2,0,1:T(8,128)S(1)} fusion(f32[864,5,128]{2,0,1:T(8,128)S(1)} %fusion.12, f32[864,4,128]{2,0,1:T(8,128)S(1)} %fusion.70, f32[4,128]{1,0:T(4,128)S(1)} %bitcast.110, f32[4,128]{1,0:T(4,128)S(1)} %bitcast.116, f32[4,128]{1,0:T(4,128)S(1)} %get-tuple-element.37, f32[4,128]{1,0:T(4,128)S(1)} %get-tuple-element.38, ...), kind=kLoop, calls=%fused_computation.116 | loop fusion | flops 13713408 | bytes 7120768 | tf_op jit(solution)/shard_map/sub | solution.py:65
  238.7 1.9 fusion.8
  240.6 2.4 minimum_multiply_fusion
  243.1 2.6 fusion.7
  245.7 0.5 fusion.68
  246.2 0.9 fusion.72
  247.2 72.7 %psum.30 = f32[5,4,128]{2,1,0:T(4,128)S(1)} all-reduce(f32[5,4,128]{2,1,0:T(4,128)S(1)} %copy.20), channel_id=1, replica_groups=mesh['vel'=16,'space'=16] {'vel'}, use_global_device_ids=true, to_apply=%region_5.6 | all-reduce | flops 2560 | bytes 20480 | tf_op jit(solution)/shard_map/psum | solution.py:85
  319.8 0.6 fusion.109
  320.5 1.1 fusion.45
  321.7 44.7 %psum.31 = f32[3,4,128]{2,1,0:T(4,128)S(1)} all-reduce(f32[3,4,128]{2,1,0:T(4,128)S(1)} %pad_maximum_fusion.6), channel_id=1, replica_groups=mesh['vel'=16,'space'=16] {'vel'}, use_global_device_ids=true, to_apply=%region_9.10 | all-reduce | flops 1536 | bytes 12288 | tf_op jit(solution)/shard_map/psum | solution.py:114
  366.4 4.3 %fusion.67 = f32[864,4,128]{2,0,1:T(8,128)S(1)} fusion(f32[864,4,128]{2,0,1:T(8,128)S(1)} %fusion.68, f32[4,128]{1,0:T(4,128)S(1)} %bitcast.119, f32[4,128]{1,0:T(4,128)S(1)} %bitcast.121, f32[4,128]{1,0:T(4,128)S(1)} %get-tuple-element.34, f32[4,128]{1,0:T(4,128)S(1)} %get-tuple-element.35, f32[4,128]{1,0:T(4,128)S(1)} %get-tuple-element.33, ...), kind=kLoop, calls=%fused_computation.112 | loop fusion | flops 12828672 | bytes 3581824 | tf_op jit(solution)/shard_map/jit(_where)/select_n | solution.py:182
  370.6 2.3 copy.28
  (59 shorter events, 0.4 us)
Async XLA Ops:
  3.5 49.8 %copy-start = (f32[864,4,128]{2,1,0:T(4,128)S(1)}, f32[864,4,128]{2,1,0:T(4,128)}, u32[]{:S(2)}) copy-start(f32[864,4,128]{2,1,0:T(4,128)} %param.2) | copy-start | bytes 5308420
  3.5 49.9 %collective-permute-start.1 = (f32[864,2,128]{2,0,1:T(8,128)}, f32[864,2,128]{2,0,1:T(8,128)}, u32[]{:S(2)}, u32[]{:S(2)}) collective-permute-start(f32[864,2,128]{2,0,1:T(8,128)} %get-tuple-element.21), channel_id=1, source_target_pairs={{1,0},{2,1},{3,2},{4,3},{5,4},{6,5},{7,6},{8,7},{9,8},{10,9},{11,1... | collective-permute-start | bytes 2654216 | tf_op jit(solution)/shard_map/ppermute | solution.py:28
  11.6 40.5 %collective-permute-start = (f32[864,2,128]{2,0,1:T(8,128)}, f32[864,2,128]{2,0,1:T(8,128)}, u32[]{:S(2)}, u32[]{:S(2)}) collective-permute-start(f32[864,2,128]{2,0,1:T(8,128)} %get-tuple-element.22), channel_id=1, source_target_pairs={{0,1},{1,2},{2,3},{3,4},{4,5},{5,6},{6,7},{7,8},{8,9},{9,10},{10,1... | collective-permute-start | bytes 2654216 | tf_op jit(solution)/shard_map/ppermute | solution.py:25
  16.2 46.4 %copy-start.3 = (f32[864]{0:T(1024)}, f32[864]{0:T(1024)S(1)}, u32[]{:S(2)}) copy-start(f32[864]{0:T(1024)S(1)} %get-tuple-element.51) | copy-start | bytes 10372
  16.2 46.4 %copy-start.5 = (f32[864]{0:T(1024)}, f32[864]{0:T(1024)S(1)}, u32[]{:S(2)}) copy-start(f32[864]{0:T(1024)S(1)} %get-tuple-element.52) | copy-start | bytes 10372
  16.3 39.8 %copy-start.13 = (f32[864]{0:T(1024)}, f32[864]{0:T(1024)S(1)}, u32[]{:S(2)}) copy-start(f32[864]{0:T(1024)S(1)} %get-tuple-element.62) | copy-start | bytes 10372
  16.3 46.4 %copy-start.7 = (f32[864]{0:T(1024)}, f32[864]{0:T(1024)S(1)}, u32[]{:S(2)}) copy-start(f32[864]{0:T(1024)S(1)} %get-tuple-element.61) | copy-start | bytes 10372
  16.9 39.1 %copy-start.15 = (pred[864]{0:T(1024)(128)(4,1)}, pred[864]{0:T(1024)(128)(4,1)S(1)}, u32[]{:S(2)}) copy-start(pred[864]{0:T(1024)(128)(4,1)S(1)} %get-tuple-element.60) | copy-start | bytes 2596
  17.0 45.7 %copy-start.17 = (pred[864]{0:T(1024)(128)(4,1)}, pred[864]{0:T(1024)(128)(4,1)S(1)}, u32[]{:S(2)}) copy-start(pred[864]{0:T(1024)(128)(4,1)S(1)} %get-tuple-element.59) | copy-start | bytes 2596
  54.9 1.2 copy-start.9
  54.9 1.2 copy-start.11
  65.3 0.7 copy-start.1
  66.0 117.4 %copy-start.2 = (f32[864]{0:T(1024)S(1)}, f32[864]{0:T(1024)}, u32[]{:S(2)}) copy-start(f32[864]{0:T(1024)} %get-tuple-element.50) | copy-start | bytes 10372
  66.0 117.4 %copy-start.19 = (pred[4,128]{1,0:T(4,128)(4,1)S(1)}, pred[4,128]{1,0:T(4,128)(4,1)}, u32[]{:S(2)}) copy-start(pred[4,128]{1,0:T(4,128)(4,1)} %get-tuple-element.45) | copy-start | bytes 1540
  66.0 117.4 %copy-start.20 = (pred[4,128]{1,0:T(4,128)(4,1)S(1)}, pred[4,128]{1,0:T(4,128)(4,1)}, u32[]{:S(2)}) copy-start(pred[4,128]{1,0:T(4,128)(4,1)} %get-tuple-element.46) | copy-start | bytes 1540
  187.8 44.4 %collective-permute-start.2 = (f32[864,2,128]{2,0,1:T(8,128)S(1)}, f32[864,2,128]{2,0,1:T(8,128)S(1)}, u32[]{:S(2)}, u32[]{:S(2)}) collective-permute-start(f32[864,2,128]{2,0,1:T(8,128)S(1)} %get-tuple-element.19), channel_id=1, source_target_pairs={{0,1},{1,2},{2,3},{3,4},{4,5},{5,6},{6,7},{7,8},{8,9},{9,10},{10,1... | collective-permute-start | bytes 2654216 | tf_op jit(solution)/shard_map/ppermute | solution.py:25
  189.8 42.4 %collective-permute-start.3 = (f32[864,2,128]{2,0,1:T(8,128)S(1)}, f32[864,2,128]{2,0,1:T(8,128)S(1)}, u32[]{:S(2)}, u32[]{:S(2)}) collective-permute-start(f32[864,2,128]{2,0,1:T(8,128)S(1)} %get-tuple-element.20), channel_id=1, source_target_pairs={{1,0},{2,1},{3,2},{4,3},{5,4},{6,5},{7,6},{8,7},{9,8},{10,9},{11,1... | collective-permute-start | bytes 2654216 | tf_op jit(solution)/shard_map/ppermute | solution.py:28
  232.7 1.2 copy-start.10
  232.7 1.2 copy-start.12
  232.7 1.2 copy-start.14
  232.7 1.2 copy-start.16
  240.6 2.5 copy-start.4
  240.6 2.5 copy-start.6
  240.6 2.5 copy-start.8
  240.6 2.5 copy-start.18
where the time goes:
time: 373 us
  blocking collectives  233 us (62%)
  waiting for transfers between devices  67.8 us (18%)
  other arithmetic  39.1 us (10%)
  starting transfers between devices  20.3 us (5%)
  local copies, waits for them, and re-layouts  10.1 us (3%)
    psum x2, blocking collectives, macroscopic_moments(): integral_totals = lax.psum(local, 'vel')  144 us
    psum x2, blocking collectives, macroscopic_moments(): conductive_transfer = lax.psum(local_heat, 'vel')  89 us
    ppermute x2, waiting for transfers between devices, with_halo(): lax.ppermute(lax.slice_in_dim(block, block.shape[dim] - width, None, axis...  67.8 us
    ppermute x2, starting transfers between devices, with_halo(): lax.ppermute(lax.slice_in_dim(block, 0, width, axis=dim), axis, backward)  16.5 us
    select_n x2, other arithmetic, approach_increment(): jnp.where(kind_labels == 1, wall_distribution, jnp.where(kind_labels == 2...  8.54 us
    mul x4, other arithmetic, sweep(): flux = number * jnp.where(number > 0, left_face, right_face)  8.15 us
  transfers between devices with their start and end apart: 4, of which 2 were waited for; matrix products, arithmetic and copies ran while one was open for 2% of the time, Pallas kernels for 0%

commit v1 on v0

--- a/solution.py
+++ b/solution.py
@@ -74,6 +74,11 @@
 
 
 def macroscopic_moments(advected_distribution, along_x_part, along_y_part, along_z_part):
+
+    def touch_axis_part_on(xx):
+        y1 = jnp.sum(lax.all_gather(xx, "vel"), axis=0)
+        return y1
+
     magnitude_squares = (
         along_x_part * along_x_part + along_y_part * along_y_part + along_z_part * along_z_part
     )
@@ -111,7 +116,7 @@
             jnp.sum(rel_z * scaled, axis=0),
         ]
     )
-    conductive_transfer = lax.psum(local_heat, "vel")
+    conductive_transfer = touch_axis_part_on(local_heat)
     return (
         particle_concentration,
         average_drift_x,

time: 373 us -> 371 us (level)
    psum x2 -> x0, blocking collectives: 89 us -> none  [macroscopic_moments(): conductive_transfer = lax.psum(local_heat, 'vel')]
    all_gather x0 -> x2, blocking collectives: none -> 86.8 us  [touch_axis_part_on(): y1 = jnp.sum(lax.all_gather(xx, 'vel'), axis=0)]
where the time goes in v1:
time: 371 us
  blocking collectives  230 us (62%)
  waiting for transfers between devices  67.8 us (18%)
  other arithmetic  39.2 us (11%)
  starting transfers between devices  20.3 us (5%)
  local copies, waits for them, and re-layouts  10.1 us (3%)
    psum x2, blocking collectives, macroscopic_moments(): integral_totals = lax.psum(local, 'vel')  143 us
    all_gather x2, blocking collectives, touch_axis_part_on(): y1 = jnp.sum(lax.all_gather(xx, 'vel'), axis=0)  86.8 us
    ppermute x2, waiting for transfers between devices, with_halo(): lax.ppermute(lax.slice_in_dim(block, block.shape[dim] - width, None, axis...  67.8 us
    ppermute x2, starting transfers between devices, with_halo(): lax.ppermute(lax.slice_in_dim(block, 0, width, axis=dim), axis, backward)  16.5 us
    select_n x2, other arithmetic, approach_increment(): jnp.where(kind_labels == 1, wall_distribution, jnp.where(kind_labels == 2...  8.54 us
    mul x4, other arithmetic, sweep(): flux = number * jnp.where(number > 0, left_face, right_face)  8.15 us
  transfers between devices with their start and end apart: 4, of which 2 were waited for; matrix products, arithmetic and copies ran while one was open for 2% of the time, Pallas kernels for 0%

profile of v1, /device:TPU:38, one launch (start us, length us, event | category | flops | bytes accessed | tf_op | source)
XLA Modules:
  0.0 370.7 jit_solution(13983804157824792558)
XLA Ops:
  0.6 1.6 copy.19
  2.2 1.3 fusion.116
  3.5 8.0 %collective-permute-start.1 = (f32[864,2,128]{2,0,1:T(8,128)}, f32[864,2,128]{2,0,1:T(8,128)}, u32[]{:S(2)}, u32[]{:S(2)}) collective-permute-start(f32[864,2,128]{2,0,1:T(8,128)} %get-tuple-element.21), channel_id=1, source_target_pairs={{1,0},{2,1},{3,2},{4,3},{5,4},{6,5},{7,6},{8,7},{9,8},{10,9},{11,1... | collective-permute-start | bytes 2654216 | tf_op jit(solution)/shard_map/ppermute | solution.py:28
  11.6 1.9 collective-permute-start
  13.5 0.1 multiply_add_fusion
  13.7 0.6 add_multiply_fusion.1
  14.3 0.6 broadcast.950
  14.9 1.3 stack.36
  16.3 0.6 multiply_exponential_fusion
  17.0 1.3 broadcast_compare_fusion.3
  18.3 33.8 %collective-permute-done = f32[864,2,128]{2,0,1:T(8,128)} collective-permute-done((f32[864,2,128]{2,0,1:T(8,128)}, f32[864,2,128]{2,0,1:T(8,128)}, u32[]{:S(2)}, u32[]{:S(2)}) %collective-permute-start) | collective-permute-done | bytes 884768 | tf_op jit(solution)/shard_map/ppermute | solution.py:25
  52.1 1.2 constant_dynamic-update-slice_fusion.2
  53.3 0.1 constant_dynamic-update-slice_fusion.1
  53.4 1.2 constant_dynamic-update-slice_fusion
  54.7 0.2 slice_subtract_fusion.1
  54.9 1.1 minimum_multiply_fusion.3
  56.1 2.0 fusion.16
  58.1 0.2 fusion.71
  58.3 1.9 fusion.3
  60.2 2.4 minimum_multiply_fusion.1
  62.7 2.6 fusion.2
  65.3 0.5 fusion.70
  65.8 0.2 copy-done.1
  66.0 0.9 fusion.74
  67.0 70.9 %psum.14 = f32[5,4,128]{2,0,1:T(8,128)S(1)} all-reduce(f32[5,4,128]{2,0,1:T(8,128)S(1)} %fusion.74), channel_id=1, replica_groups=mesh['vel'=16,'space'=16] {'vel'}, use_global_device_ids=true, to_apply=%region_0.1 | all-reduce | flops 2560 | bytes 20480 | tf_op jit(solution)/shard_map/psum | solution.py:90
  137.9 1.1 fusion.20
  139.1 43.2 %all-gather = f32[48,4,128]{2,1,0:T(4,128)S(1)} all-gather(f32[3,4,128]{2,1,0:T(4,128)S(1)} %pad_maximum_fusion.5), channel_id=2, replica_groups=mesh['vel'=16,'space'=16] {'vel'}, dimensions={0}, use_global_device_ids=true | all-gather | bytes 104448 | tf_op jit(solution)/shard_map/all_gather | solution.py:79
  182.4 4.3 %fusion.42 = f32[864,4,128]{2,0,1:T(8,128)S(1)} fusion(f32[864,4,128]{2,0,1:T(8,128)S(1)} %fusion.70, f32[4,128]{1,0:T(4,128)S(1)} %bitcast.113, f32[4,128]{1,0:T(4,128)S(1)} %bitcast.119, f32[4,128]{1,0:T(4,128)S(1)} %get-tuple-element.37, f32[4,128]{1,0:T(4,128)S(1)} %get-tuple-element.38, f32[4,128]{1,0:T(4,128)S(1)} %get-tuple-element.36, ...), kind=kLoop, calls=%fused_computation.87 | loop fusion | flops 12828672 | bytes 3581824 | tf_op jit(solution)/shard_map/jit(_where)/select_n | solution.py:187
  186.6 0.1 fusion.115
  186.8 1.9 collective-permute-start.2
  188.7 8.4 %collective-permute-start.3 = (f32[864,2,128]{2,0,1:T(8,128)S(1)}, f32[864,2,128]{2,0,1:T(8,128)S(1)}, u32[]{:S(2)}, u32[]{:S(2)}) collective-permute-start(f32[864,2,128]{2,0,1:T(8,128)S(1)} %get-tuple-element.20), channel_id=1, source_target_pairs={{1,0},{2,1},{3,2},{4,3},{5,4},{6,5},{7,6},{8,7},{9,8},{10,9},{11,1... | collective-permute-start | bytes 2654216 | tf_op jit(solution)/shard_map/ppermute | solution.py:28
  197.2 34.0 %collective-permute-done.2 = f32[864,2,128]{2,0,1:T(8,128)S(1)} collective-permute-done((f32[864,2,128]{2,0,1:T(8,128)S(1)}, f32[864,2,128]{2,0,1:T(8,128)S(1)}, u32[]{:S(2)}, u32[]{:S(2)}) %collective-permute-start.2) | collective-permute-done | bytes 884768 | tf_op jit(solution)/shard_map/ppermute | solution.py:25
  231.2 0.2 pad_maximum_fusion
  231.4 0.2 slice_subtract_fusion
  231.7 1.1 minimum_multiply_fusion.2
  232.9 1.0 fusion.12
  233.8 3.8 %fusion.69 = f32[864,4,128]{2,0,1:T(8,128)S(1)} fusion(f32[864,5,128]{2,0,1:T(8,128)S(1)} %fusion.12, f32[864,4,128]{2,0,1:T(8,128)S(1)} %fusion.70, f32[4,128]{1,0:T(4,128)S(1)} %bitcast.114, f32[4,128]{1,0:T(4,128)S(1)} %bitcast.120, f32[4,128]{1,0:T(4,128)S(1)} %get-tuple-element.37, f32[4,128]{1,0:T(4,128)S(1)} %get-tuple-element.38, ...), kind=kLoop, calls=%fused_computation.116 | loop fusion | flops 13713408 | bytes 7120768 | tf_op jit(solution)/shard_map/sub | solution.py:65
  237.7 1.9 fusion.8
  239.6 2.4 minimum_multiply_fusion
  242.1 2.6 fusion.7
  244.7 0.5 fusion.68
  245.2 0.9 fusion.72
  246.1 72.5 %psum.15 = f32[5,4,128]{2,1,0:T(4,128)S(1)} all-reduce(f32[5,4,128]{2,1,0:T(4,128)S(1)} %copy.20), channel_id=1, replica_groups=mesh['vel'=16,'space'=16] {'vel'}, use_global_device_ids=true, to_apply=%region_5.6 | all-reduce | flops 2560 | bytes 20480 | tf_op jit(solution)/shard_map/psum | solution.py:90
  318.6 0.6 fusion.109
  319.3 1.1 fusion.45
  320.5 43.6 %all-gather.1 = f32[48,4,128]{2,1,0:T(4,128)S(1)} all-gather(f32[3,4,128]{2,1,0:T(4,128)S(1)} %pad_maximum_fusion.6), channel_id=3, replica_groups=mesh['vel'=16,'space'=16] {'vel'}, dimensions={0}, use_global_device_ids=true | all-gather | bytes 104448 | tf_op jit(solution)/shard_map/all_gather | solution.py:79
  364.1 4.3 %fusion.67 = f32[864,4,128]{2,0,1:T(8,128)S(1)} fusion(f32[864,4,128]{2,0,1:T(8,128)S(1)} %fusion.68, f32[4,128]{1,0:T(4,128)S(1)} %bitcast.123, f32[4,128]{1,0:T(4,128)S(1)} %bitcast.125, f32[4,128]{1,0:T(4,128)S(1)} %get-tuple-element.34, f32[4,128]{1,0:T(4,128)S(1)} %get-tuple-element.35, f32[4,128]{1,0:T(4,128)S(1)} %get-tuple-element.33, ...), kind=kLoop, calls=%fused_computation.112 | loop fusion | flops 12828672 | bytes 3581824 | tf_op jit(solution)/shard_map/jit(_where)/select_n | solution.py:187
  368.3 2.3 copy.28
  (61 shorter events, 0.5 us)
Async XLA Ops:
  3.5 49.8 %copy-start = (f32[864,4,128]{2,1,0:T(4,128)S(1)}, f32[864,4,128]{2,1,0:T(4,128)}, u32[]{:S(2)}) copy-start(f32[864,4,128]{2,1,0:T(4,128)} %param.2) | copy-start | bytes 5308420
  3.5 49.9 %collective-permute-start.1 = (f32[864,2,128]{2,0,1:T(8,128)}, f32[864,2,128]{2,0,1:T(8,128)}, u32[]{:S(2)}, u32[]{:S(2)}) collective-permute-start(f32[864,2,128]{2,0,1:T(8,128)} %get-tuple-element.21), channel_id=1, source_target_pairs={{1,0},{2,1},{3,2},{4,3},{5,4},{6,5},{7,6},{8,7},{9,8},{10,9},{11,1... | collective-permute-start | bytes 2654216 | tf_op jit(solution)/shard_map/ppermute | solution.py:28
  11.6 40.5 %collective-permute-start = (f32[864,2,128]{2,0,1:T(8,128)}, f32[864,2,128]{2,0,1:T(8,128)}, u32[]{:S(2)}, u32[]{:S(2)}) collective-permute-start(f32[864,2,128]{2,0,1:T(8,128)} %get-tuple-element.22), channel_id=1, source_target_pairs={{0,1},{1,2},{2,3},{3,4},{4,5},{5,6},{6,7},{7,8},{8,9},{9,10},{10,1... | collective-permute-start | bytes 2654216 | tf_op jit(solution)/shard_map/ppermute | solution.py:25
  16.2 46.4 %copy-start.3 = (f32[864]{0:T(1024)}, f32[864]{0:T(1024)S(1)}, u32[]{:S(2)}) copy-start(f32[864]{0:T(1024)S(1)} %get-tuple-element.51) | copy-start | bytes 10372
  16.2 46.4 %copy-start.5 = (f32[864]{0:T(1024)}, f32[864]{0:T(1024)S(1)}, u32[]{:S(2)}) copy-start(f32[864]{0:T(1024)S(1)} %get-tuple-element.52) | copy-start | bytes 10372
  16.3 39.8 %copy-start.13 = (f32[864]{0:T(1024)}, f32[864]{0:T(1024)S(1)}, u32[]{:S(2)}) copy-start(f32[864]{0:T(1024)S(1)} %get-tuple-element.62) | copy-start | bytes 10372
  16.3 46.4 %copy-start.7 = (f32[864]{0:T(1024)}, f32[864]{0:T(1024)S(1)}, u32[]{:S(2)}) copy-start(f32[864]{0:T(1024)S(1)} %get-tuple-element.61) | copy-start | bytes 10372
  16.9 39.1 %copy-start.15 = (pred[864]{0:T(1024)(128)(4,1)}, pred[864]{0:T(1024)(128)(4,1)S(1)}, u32[]{:S(2)}) copy-start(pred[864]{0:T(1024)(128)(4,1)S(1)} %get-tuple-element.60) | copy-start | bytes 2596
  17.0 45.7 %copy-start.17 = (pred[864]{0:T(1024)(128)(4,1)}, pred[864]{0:T(1024)(128)(4,1)S(1)}, u32[]{:S(2)}) copy-start(pred[864]{0:T(1024)(128)(4,1)S(1)} %get-tuple-element.59) | copy-start | bytes 2596
  54.9 1.2 copy-start.9
  54.9 1.2 copy-start.11
  65.3 0.7 copy-start.1
  66.0 116.3 %copy-start.2 = (f32[864]{0:T(1024)S(1)}, f32[864]{0:T(1024)}, u32[]{:S(2)}) copy-start(f32[864]{0:T(1024)} %get-tuple-element.50) | copy-start | bytes 10372
  66.0 116.3 %copy-start.19 = (pred[4,128]{1,0:T(4,128)(4,1)S(1)}, pred[4,128]{1,0:T(4,128)(4,1)}, u32[]{:S(2)}) copy-start(pred[4,128]{1,0:T(4,128)(4,1)} %get-tuple-element.45) | copy-start | bytes 1540
  66.0 116.3 %copy-start.20 = (pred[4,128]{1,0:T(4,128)(4,1)S(1)}, pred[4,128]{1,0:T(4,128)(4,1)}, u32[]{:S(2)}) copy-start(pred[4,128]{1,0:T(4,128)(4,1)} %get-tuple-element.46) | copy-start | bytes 1540
  186.8 44.4 %collective-permute-start.2 = (f32[864,2,128]{2,0,1:T(8,128)S(1)}, f32[864,2,128]{2,0,1:T(8,128)S(1)}, u32[]{:S(2)}, u32[]{:S(2)}) collective-permute-start(f32[864,2,128]{2,0,1:T(8,128)S(1)} %get-tuple-element.19), channel_id=1, source_target_pairs={{0,1},{1,2},{2,3},{3,4},{4,5},{5,6},{6,7},{7,8},{8,9},{9,10},{10,1... | collective-permute-start | bytes 2654216 | tf_op jit(solution)/shard_map/ppermute | solution.py:25
  188.7 42.5 %collective-permute-start.3 = (f32[864,2,128]{2,0,1:T(8,128)S(1)}, f32[864,2,128]{2,0,1:T(8,128)S(1)}, u32[]{:S(2)}, u32[]{:S(2)}) collective-permute-start(f32[864,2,128]{2,0,1:T(8,128)S(1)} %get-tuple-element.20), channel_id=1, source_target_pairs={{1,0},{2,1},{3,2},{4,3},{5,4},{6,5},{7,6},{8,7},{9,8},{10,9},{11,1... | collective-permute-start | bytes 2654216 | tf_op jit(solution)/shard_map/ppermute | solution.py:28
  231.6 1.2 copy-start.10
  231.6 1.2 copy-start.12
  231.6 1.2 copy-start.14
  231.7 1.2 copy-start.16
  239.6 2.5 copy-start.4
  239.6 2.5 copy-start.6
  239.6 2.5 copy-start.8
  239.6 2.5 copy-start.18
